TPU v7x, 512 devices: a whole 4x8x8 slice. The times are simulated.
512 devices in a mesh: dp: 8 (over x, y_hi), seq: 64 (over z, y_lo, core).
Axes of the slice: x: 4, y: 8 (y_hi: 2, y_lo: 4; y = y_hi * 4 + y_lo), z: 8, core: 2. Of those that a mesh axis runs over, the one named last changes fastest.
Arguments:
- tokens: bfloat16 [8, 128, 256, 768], P('dp', 'seq'), may hold values from -6 to 6
- upstream: bfloat16 [8, 128, 256, 768], P('dp', 'seq'), may hold values from -0.078125 to 0.078125
- row_factor: bfloat16 [128, 256, 256], P('seq'), may hold values from -0.375 to 0.375
- column_factor: bfloat16 [256, 128, 128], P('seq'), may hold values from -0.5 to 0.5
Outputs:
- grad_row: bfloat16 [128, 256, 256], P('seq')
- grad_column: bfloat16 [256, 128, 128], P('seq')
All inputs are finite; a program needn't handle non-finite values.
Results may differ from a plain program's by a relative error of at most 0.005.
Values may be sent and summed in bfloat16 or wider, within the bound.
No kernel may reach another device: no remote copies, remote signals or barrier semaphores. Data moves between devices by JAX's collectives and lax.ppermute only.
A program may use at most 64 MiB of HBM per device.

v0:
```python
import jax
import jax.numpy as jnp
from jax import lax
from jax.sharding import PartitionSpec as P


def apply_rows(row_factor, tokens):
    return jnp.einsum(
        "rij,brjd->brid", row_factor, tokens, preferred_element_type=jnp.float32
    ).astype(jnp.bfloat16)


def shards(tokens, upstream, row_factor, column_factor):
    mixed = apply_rows(row_factor, tokens)
    mixed_cols, upstream_cols = (
        lax.all_to_all(mixed, "seq", split_axis=2, concat_axis=1, tiled=True),
        lax.all_to_all(upstream, "seq", split_axis=2, concat_axis=1, tiled=True),
    )
    sum_column = jnp.einsum(
        "brcd,bscd->crs", upstream_cols, mixed_cols, preferred_element_type=jnp.float32
    )
    back_cols = jnp.einsum(
        "crs,brcd->bscd", column_factor, upstream_cols, preferred_element_type=jnp.float32
    ).astype(jnp.bfloat16)
    back_rows = lax.all_to_all(back_cols, "seq", split_axis=1, concat_axis=2, tiled=True)
    sum_row = jnp.einsum("brid,brjd->rij", back_rows, tokens, preferred_element_type=jnp.float32)
    total_row, total_column = lax.psum((sum_row, sum_column), "dp")
    return (total_row.astype(jnp.bfloat16), total_column.astype(jnp.bfloat16))


def solution(mesh):
    placed = (
        P("dp", "seq", None, None),
        P("dp", "seq", None, None),
        P("seq", None, None),
        P("seq", None, None),
    )
    return jax.shard_map(
        shards,
        mesh=mesh,
        in_specs=placed,
        out_specs=(P("seq", None, None), P("seq", None, None)),
        check_vma=False,
    )
```

profile of v0, /device:TPU:8, one launch (start us, length us, event | category | flops | bytes accessed | tf_op | source)
XLA Modules:
  0.0 184.0 jit_solution(4781632481716380268)
XLA Ops:
  0.6 0.0 copy-start
  0.6 2.9 %copy.21 = bf16[1,2,256,768]{3,1,0,2:T(2,128)(2,1)} copy(bf16[1,2,256,768]{3,2,1,0:T(8,128)(2,1)} %param.5) | data formatting | bytes 1572864 | tf_op args[1]
  3.5 0.0 copy-start.3
  3.5 14.5 %all-to-all-start = ((bf16[1,2,256,768]{3,1,0,2:T(2,128)(2,1)}), bf16[1,2,256,768]{3,1,0,2:T(2,128)(2,1)S(1)}, u32[]{:S(2)}, u32[]{:S(2)}) async-start(bf16[1,2,256,768]{3,1,0,2:T(2,128)(2,1)} %copy.21), calls=%async_computation | async-start | bytes 1572864 | tf_op jit(solution)/shard_map/all_to_all | solution.py:17
  18.0 0.0 copy-done
  18.1 0.0 copy-done.3
  18.1 0.4 fusion.1
  18.5 1.9 %copy.27 = bf16[1,2,256,768]{3,1,0,2:T(2,128)(2,1)} copy(bf16[1,2,256,768]{2,3,1,0:T(8,128)(2,1)S(1)} %fusion.1) | data formatting | bytes 1572864 | tf_op jit(solution)/shard_map/convert_element_type | solution.py:10
  20.4 21.2 %all-to-all-done = bf16[1,2,256,768]{3,1,0,2:T(2,128)(2,1)S(1)} async-done(((bf16[1,2,256,768]{3,1,0,2:T(2,128)(2,1)}), bf16[1,2,256,768]{3,1,0,2:T(2,128)(2,1)S(1)}, u32[]{:S(2)}, u32[]{:S(2)}) %all-to-all-start) | async-done | bytes 786464 | tf_op jit(solution)/shard_map/all_to_all | solution.py:17
  41.6 5.4 %all-to-all-start.2 = ((bf16[1,2,256,768]{3,1,0,2:T(2,128)(2,1)}), bf16[1,2,256,768]{3,1,0,2:T(2,128)(2,1)S(1)}, u32[]{:S(2)}, u32[]{:S(2)}) async-start(bf16[1,2,256,768]{3,1,0,2:T(2,128)(2,1)} %copy.27), calls=%async_computation.2 | async-start | bytes 1572864 | tf_op jit(solution)/shard_map/all_to_all | solution.py:16
  47.0 0.0 copy-start.4
  47.0 0.3 copy.22
  47.4 0.0 copy-start.1
  47.4 0.9 copy-done.1
  48.2 0.0 copy-done.4
  48.2 0.4 fusion
  48.7 1.3 copy.24
  50.0 20.6 %all-to-all-done.2 = bf16[1,2,256,768]{3,1,0,2:T(2,128)(2,1)S(1)} async-done(((bf16[1,2,256,768]{3,1,0,2:T(2,128)(2,1)}), bf16[1,2,256,768]{3,1,0,2:T(2,128)(2,1)S(1)}, u32[]{:S(2)}, u32[]{:S(2)}) %all-to-all-start.2) | async-done | bytes 786464 | tf_op jit(solution)/shard_map/all_to_all | solution.py:16
  70.6 5.4 %all-to-all-start.1 = ((bf16[1,128,4,768]{3,2,0,1:T(4,128)(2,1)}), bf16[1,128,4,768]{3,2,0,1:T(4,128)(2,1)S(1)}, u32[]{:S(2)}, u32[]{:S(2)}) async-start(bf16[1,128,4,768]{3,2,0,1:T(4,128)(2,1)} %copy.24), calls=%async_computation.1 | async-start | bytes 1572864 | tf_op jit(solution)/shard_map/all_to_all | solution.py:25
  76.0 0.5 copy.28
  76.6 0.0 copy-start.2
  76.6 1.2 reshape.29
  77.8 0.0 copy-done.2
  77.8 1.5 convolution_bitcast_fusion
  79.3 20.3 %all-to-all-done.1 = bf16[1,128,4,768]{3,2,0,1:T(4,128)(2,1)S(1)} async-done(((bf16[1,128,4,768]{3,2,0,1:T(4,128)(2,1)}), bf16[1,128,4,768]{3,2,0,1:T(4,128)(2,1)S(1)}, u32[]{:S(2)}, u32[]{:S(2)}) %all-to-all-start.1) | async-done | bytes 786464 | tf_op jit(solution)/shard_map/all_to_all | solution.py:25
  99.5 0.3 copy.25
  99.8 0.2 reshape.27
  100.0 0.4 fusion.3
  100.4 82.8 %all-reduce.2 = (bf16[2,256,256]{2,1,0:T(8,128)(2,1)}, bf16[4,128,128]{1,2,0:T(8,128)(2,1)S(1)}) all-reduce(f32[2,256,256]{2,1,0:T(8,128)S(1)} %fusion.3, f32[4,128,128]{1,2,0:T(8,128)S(1)} %convolution_bitcast_fusion), channel_id=1, replica_groups=mesh['dp'=8,'seq'=64] {'dp'}, use_global_device_ids=true, to_apply=%region_0.0 | all-reduce | flops 196608 | bytes 1179648 | tf_op jit(solution)/shard_map/psum | solution.py:27
  183.2 0.8 copy.30
Async XLA Ops:
  0.6 17.4 %copy-start = (bf16[1,2,256,768]{3,2,1,0:T(8,128)(2,1)S(1)}, bf16[1,2,256,768]{3,2,1,0:T(8,128)(2,1)}, u32[]{:S(2)}) copy-start(bf16[1,2,256,768]{3,2,1,0:T(8,128)(2,1)} %param.4) | copy-start | bytes 2359300
  3.5 14.5 %copy-start.3 = (bf16[2,256,256]{2,1,0:T(8,128)(2,1)S(1)}, bf16[2,256,256]{2,1,0:T(8,128)(2,1)}, u32[]{:S(2)}) copy-start(bf16[2,256,256]{2,1,0:T(8,128)(2,1)} %param.6) | copy-start | bytes 786436
  3.5 38.0 %all-to-all-start = ((bf16[1,2,256,768]{3,1,0,2:T(2,128)(2,1)}), bf16[1,2,256,768]{3,1,0,2:T(2,128)(2,1)S(1)}, u32[]{:S(2)}, u32[]{:S(2)}) async-start(bf16[1,2,256,768]{3,1,0,2:T(2,128)(2,1)} %copy.21), calls=%async_computation | async-start | bytes 1572864 | tf_op jit(solution)/shard_map/all_to_all | solution.py:17
  41.6 29.0 %all-to-all-start.2 = ((bf16[1,2,256,768]{3,1,0,2:T(2,128)(2,1)}), bf16[1,2,256,768]{3,1,0,2:T(2,128)(2,1)S(1)}, u32[]{:S(2)}, u32[]{:S(2)}) async-start(bf16[1,2,256,768]{3,1,0,2:T(2,128)(2,1)} %copy.27), calls=%async_computation.2 | async-start | bytes 1572864 | tf_op jit(solution)/shard_map/all_to_all | solution.py:16
  47.0 1.2 copy-start.4
  47.4 0.9 copy-start.1
  70.6 29.0 %all-to-all-start.1 = ((bf16[1,128,4,768]{3,2,0,1:T(4,128)(2,1)}), bf16[1,128,4,768]{3,2,0,1:T(4,128)(2,1)S(1)}, u32[]{:S(2)}, u32[]{:S(2)}) async-start(bf16[1,128,4,768]{3,2,0,1:T(4,128)(2,1)} %copy.24), calls=%async_computation.1 | async-start | bytes 1572864 | tf_op jit(solution)/shard_map/all_to_all | solution.py:25
  76.6 1.2 copy-start.2
where the time goes:
time: 184 us
  blocking collectives  82.8 us (45%)
  waiting for transfers between devices  62.1 us (34%)
  starting transfers between devices  25.4 us (14%)
  local copies, waits for them, and re-layouts  10.2 us (6%)
  matrix products  2.77 us (2%)
    psum x1, blocking collectives, shards(): total_row, total_column = lax.psum((sum_row, sum_column), 'dp')  82.8 us
    all_to_all x1, waiting for transfers between devices, shards(): lax.all_to_all(upstream, 'seq', split_axis=2, concat_axis=1, tiled=True)  21.2 us
    all_to_all x1, waiting for transfers between devices, shards(): lax.all_to_all(mixed, 'seq', split_axis=2, concat_axis=1, tiled=True)  20.6 us
    all_to_all x1, waiting for transfers between devices, shards(): lax.all_to_all(back_cols, 'seq', split_axis=1, concat_axis=2, tiled=True)  20.3 us
    all_to_all x1, starting transfers between devices, shards(): lax.all_to_all(upstream, 'seq', split_axis=2, concat_axis=1, tiled=True)  14.5 us
    all_to_all x1, starting transfers between devices, shards(): lax.all_to_all(mixed, 'seq', split_axis=2, concat_axis=1, tiled=True)  5.44 us
    all_to_all x1, starting transfers between devices, shards(): lax.all_to_all(back_cols, 'seq', split_axis=1, concat_axis=2, tiled=True)  5.44 us
    unnamed x12, local copies, waits for them, and re-layouts  4.56 us
  transfers between devices with their start and end apart: 3, of which 3 were waited for; matrix products, arithmetic and copies ran while one was open for 4% of the time, Pallas kernels for 0%

commit v1 on v0

v1 whole, which is shorter than its diff:
```python
import jax
import jax.numpy as jnp
from jax import lax
from jax.sharding import PartitionSpec as P


def apply_rows(row_factor, tokens):
    return jnp.einsum(
        "rij,brjd->brid", row_factor, tokens, preferred_element_type=jnp.float32
    ).astype(jnp.bfloat16)


def reduce_docs(flat, n):
    mine = lax.all_to_all(flat.reshape(n, -1), "dp", 0, 0, tiled=True).sum(0)
    mine = mine.astype(jnp.bfloat16)
    spread = jnp.broadcast_to(mine[None], (n, mine.shape[0]))
    return lax.all_to_all(spread, "dp", 0, 0, tiled=True).reshape(-1)


def shards(tokens, upstream, row_factor, column_factor):
    n = lax.psum(1, "dp")
    k = lax.psum(1, "seq")
    _, rows, cols, d = tokens.shape
    mixed = apply_rows(row_factor, tokens)
    upstream_cols = lax.all_to_all(upstream, "seq", split_axis=2, concat_axis=1, tiled=True)
    back_cols = jnp.einsum(
        "crs,brcd->bscd", column_factor, upstream_cols, preferred_element_type=jnp.float32
    ).astype(jnp.bfloat16)
    ncol = cols // k
    send_m = mixed[0].reshape(rows, k, ncol, d).transpose(1, 0, 2, 3)
    send_b = back_cols[0].reshape(k, rows, ncol, d)
    got = lax.all_to_all(jnp.stack([send_m, send_b], 1), "seq", 0, 0, tiled=True)
    mixed_cols = got[:, 0].reshape(1, k * rows, ncol, d)
    back_rows = got[:, 1].transpose(1, 0, 2, 3).reshape(1, rows, cols, d)
    sum_column = jnp.einsum(
        "brcd,bscd->crs", upstream_cols, mixed_cols, preferred_element_type=jnp.float32
    )
    sum_row = jnp.einsum("brid,brjd->rij", back_rows, tokens, preferred_element_type=jnp.float32)
    flat = jnp.concatenate([sum_row.reshape(-1), sum_column.reshape(-1)])
    total = reduce_docs(flat, n)
    split = sum_row.size
    return (total[:split].reshape(sum_row.shape), total[split:].reshape(sum_column.shape))


def solution(mesh):
    placed = (
        P("dp", "seq", None, None),
        P("dp", "seq", None, None),
        P("seq", None, None),
        P("seq", None, None),
    )
    return jax.shard_map(
        shards,
        mesh=mesh,
        in_specs=placed,
        out_specs=(P("seq", None, None), P("seq", None, None)),
        check_vma=False,
    )
```

time: 184 us -> 151 us (0.82)
  waiting for transfers between devices: 62.1 us -> 21.8 us
  blocking collectives: 82.8 us -> 94 us
  starting transfers between devices: 25.4 us -> 14.4 us
  other arithmetic: 0 us -> 7.15 us
    all_to_all x0 -> x3, blocking collectives: none -> 94 us  [the longest x1 44.8 us: shards(): lax.all_to_all(jnp.stack([send_m, send_b], 1), 'seq', 0, 0, tiled=True)]
    psum x1 -> x0, blocking collectives: 82.8 us -> none  [shards(): total_row, total_column = lax.psum((sum_row, sum_column), 'dp')]
    all_to_all x2 -> x0, waiting for transfers between devices: 40.9 us -> none  [the longest x1 20.6 us: shards(): lax.all_to_all(mixed, 'seq', split_axis=2, concat_axis=1, tiled=True)]
    all_to_all x2 -> x0, starting transfers between devices: 10.9 us -> none  [the longest x1 5.44 us: shards(): lax.all_to_all(mixed, 'seq', split_axis=2, concat_axis=1, tiled=True)]
    convert_element_type x2 -> x0, local copies, waits for them, and re-layouts: 3.14 us -> none  [the longest x1 1.86 us: apply_rows(): return jnp.einsum('rij,brjd->brid', row_factor, tokens, preferred_element...]
    broadcast_in_dim x0 -> x1, other arithmetic: none -> 3 us  [reduce_docs(): spread = jnp.broadcast_to(mine[None], (n, mine.shape[0]))]
    all_to_all x0 -> x1, other arithmetic: none -> 2.36 us  [reduce_docs(): return lax.all_to_all(spread, 'dp', 0, 0, tiled=True).reshape(-1)]
  transfers between devices with their start and end apart: 3 -> 1, of which waited for: 3 -> 1; matrix products, arithmetic and copies ran while one was open for 4% -> 1% of each run, Pallas kernels for 0% -> 0%
where the time goes in v1:
time: 151 us; the launch traced here: 150 us
  blocking collectives  94 us (62%)
  waiting for transfers between devices  21.8 us (14%)
  starting transfers between devices  14.4 us (10%)
  local copies, waits for them, and re-layouts  10.6 us (7%)
  other arithmetic  7.15 us (5%)
  matrix products  1.55 us (1%)
    all_to_all x1, blocking collectives, shards(): lax.all_to_all(jnp.stack([send_m, send_b], 1), 'seq', 0, 0, tiled=True)  44.8 us
    all_to_all x1, blocking collectives, reduce_docs(): mine = lax.all_to_all(flat.reshape(n, -1), 'dp', 0, 0, tiled=True).sum(0)  32.7 us
    all_to_all x1, waiting for transfers between devices, shards(): lax.all_to_all(upstream, 'seq', split_axis=2, concat_axis=1, tiled=True)  21.8 us
    all_to_all x1, blocking collectives, reduce_docs(): return lax.all_to_all(spread, 'dp', 0, 0, tiled=True).reshape(-1)  16.5 us
    all_to_all x1, starting transfers between devices, shards(): lax.all_to_all(upstream, 'seq', split_axis=2, concat_axis=1, tiled=True)  14.4 us
    unnamed x12, local copies, waits for them, and re-layouts  4 us
  transfers between devices with their start and end apart: 1, of which 1 were waited for; matrix products, arithmetic and copies ran while one was open for 1% of the time, Pallas kernels for 0%

profile of v1, /device:TPU:8, one launch (start us, length us, event | category | flops | bytes accessed | tf_op | source)
XLA Modules:
  0.0 150.3 jit_solution(3841723803374449504)
XLA Ops:
  0.6 0.0 copy-start
  0.6 0.0 copy-start.2
  0.7 2.9 %copy.40 = bf16[1,2,256,768]{3,1,0,2:T(2,128)(2,1)} copy(bf16[1,2,256,768]{3,2,1,0:T(8,128)(2,1)} %param.5) | data formatting | bytes 1572864 | tf_op args[1]
  3.6 14.4 %all-to-all-start = ((bf16[1,2,256,768]{3,1,0,2:T(2,128)(2,1)}), bf16[1,2,256,768]{3,1,0,2:T(2,128)(2,1)S(1)}, u32[]{:S(2)}, u32[]{:S(2)}) async-start(bf16[1,2,256,768]{3,1,0,2:T(2,128)(2,1)} %copy.40), calls=%async_computation | async-start | bytes 1572864 | tf_op jit(solution)/shard_map/all_to_all | solution.py:25
  17.9 0.0 copy-done
  17.9 0.0 copy-done.2
  17.9 0.4 fusion.1
  18.3 0.2 reshape_squeeze.4
  18.5 1.2 copy.58
  19.7 21.8 %all-to-all-done = bf16[1,2,256,768]{3,1,0,2:T(2,128)(2,1)S(1)} async-done(((bf16[1,2,256,768]{3,1,0,2:T(2,128)(2,1)}), bf16[1,2,256,768]{3,1,0,2:T(2,128)(2,1)S(1)}, u32[]{:S(2)}, u32[]{:S(2)}) %all-to-all-start) | async-done | bytes 786464 | tf_op jit(solution)/shard_map/all_to_all | solution.py:25
  41.5 0.0 copy-start.3
  41.5 0.5 copy.57
  42.0 0.3 reshape.55
  42.3 0.1 copy-done.3
  42.4 0.0 copy-start.1
  42.4 0.4 fusion
  42.8 0.6 copy.49
  43.4 0.1 copy-done.1
  43.5 1.0 pad_maximum_fusion
  44.5 44.8 %all_to_all.35 = bf16[64,2,2,4,768]{4,3,2,1,0:T(4,128)(2,1)S(1)} all-to-all(bf16[64,2,2,4,768]{4,3,2,1,0:T(4,128)(2,1)S(1)} %pad_maximum_fusion), channel_id=1, replica_groups=mesh['dp'=8,'seq'=64] {'seq'}, dimensions={0} | all-to-all | bytes 3145728 | tf_op jit(solution)/shard_map/all_to_all | solution.py:32
  89.3 0.5 slice_bitcast_fusion
  89.9 0.4 convolution_bitcast_fusion
  90.2 0.1 copy.46
  90.4 0.3 copy.44
  90.7 0.2 reshape.56
  90.8 0.4 fusion.3
  91.3 0.3 copy.52
  91.5 0.1 pad_maximum_fusion.1
  91.6 32.7 %all_to_all.36 = f32[8,1,24576]{2,1,0:T(1,128)S(1)} all-to-all(f32[8,1,24576]{2,1,0:T(1,128)S(1)} %bitcast.44), channel_id=1, replica_groups=mesh['dp'=8,'seq'=64] {'dp'}, dimensions={0} | all-to-all | bytes 1572864 | tf_op jit(solution)/shard_map/all_to_all | solution.py:14
  124.3 0.7 reduce_sum.9
  125.0 0.4 broadcast_in_dim.2
  125.4 0.5 broadcast.7
  125.9 3.0 %reduce.3 = bf16[8,24576]{1,0:T(8,128)(2,1)S(1)} reduce(bf16[8,1,24576]{2,1,0:T(2,128)(2,1)S(1)} %broadcast_in_dim.2, bf16[]{:T(256)} %broadcast.7), dimensions={1}, to_apply=%broadcast_in_dim.2.reduce_sub_computation | reduce | bytes 786434 | tf_op jit(solution)/shard_map/broadcast_in_dim | solution.py:16
  128.9 0.3 reshape.62
  129.2 16.5 %all_to_all.37 = bf16[8,2,12288]{2,1,0:T(2,128)(2,1)S(1)} all-to-all(bf16[8,2,12288]{2,1,0:T(2,128)(2,1)S(1)} %reshape.62), channel_id=1, replica_groups=mesh['dp'=8,'seq'=64] {'dp'}, dimensions={0} | all-to-all | bytes 786432 | tf_op jit(solution)/shard_map/all_to_all | solution.py:17
  145.7 0.4 reshape.63
  146.1 2.4 %reduce.1 = bf16[8,24576]{1,0:T(8,128)(2,1)S(1)} reduce(bf16[8,1,24576]{2,1,0:T(2,128)(2,1)S(1)} %reshape.63, bf16[]{:T(256)} %constant.6), dimensions={1}, to_apply=%all_to_all.30.reduce_sub_computation | reduce | bytes 786434 | tf_op jit(solution)/shard_map/all_to_all | solution.py:17
  148.5 0.2 slice.20
  148.7 0.2 slice.22
  148.9 0.7 slice.26
  149.6 0.7 slice.27
Async XLA Ops:
  0.6 17.3 %copy-start = (bf16[1,2,256,768]{3,2,1,0:T(8,128)(2,1)S(1)}, bf16[1,2,256,768]{3,2,1,0:T(8,128)(2,1)}, u32[]{:S(2)}) copy-start(bf16[1,2,256,768]{3,2,1,0:T(8,128)(2,1)} %param.4) | copy-start | bytes 2359300
  0.6 17.3 %copy-start.2 = (bf16[2,256,256]{2,1,0:T(8,128)(2,1)S(1)}, bf16[2,256,256]{2,1,0:T(8,128)(2,1)}, u32[]{:S(2)}) copy-start(bf16[2,256,256]{2,1,0:T(8,128)(2,1)} %param.6) | copy-start | bytes 786436
  3.6 37.9 %all-to-all-start = ((bf16[1,2,256,768]{3,1,0,2:T(2,128)(2,1)}), bf16[1,2,256,768]{3,1,0,2:T(2,128)(2,1)S(1)}, u32[]{:S(2)}, u32[]{:S(2)}) async-start(bf16[1,2,256,768]{3,1,0,2:T(2,128)(2,1)} %copy.40), calls=%async_computation | async-start | bytes 1572864 | tf_op jit(solution)/shard_map/all_to_all | solution.py:25
  41.5 0.9 copy-start.3
  42.4 1.1 copy-start.1

commit v2 on v1

--- a/solution.py
+++ b/solution.py
@@ -10,11 +10,15 @@
     ).astype(jnp.bfloat16)
 
 
-def reduce_docs(flat, n):
-    mine = lax.all_to_all(flat.reshape(n, -1), "dp", 0, 0, tiled=True).sum(0)
-    mine = mine.astype(jnp.bfloat16)
-    spread = jnp.broadcast_to(mine[None], (n, mine.shape[0]))
-    return lax.all_to_all(spread, "dp", 0, 0, tiled=True).reshape(-1)
+def reduce_docs(sum_row, sum_column, n):
+    rows = sum_row.reshape(n, -1, sum_row.shape[-1])
+    cols = sum_column.reshape(n, -1, sum_row.shape[-1])
+    flat = jnp.concatenate([rows, cols], axis=1)
+    mine = lax.all_to_all(flat, "dp", 0, 0, tiled=True).sum(0).astype(jnp.bfloat16)
+    spread = jnp.broadcast_to(mine[None], (n,) + mine.shape)
+    total = lax.all_to_all(spread, "dp", 0, 0, tiled=True)
+    split = rows.shape[1]
+    return (total[:, :split].reshape(sum_row.shape), total[:, split:].reshape(sum_column.shape))
 
 
 def shards(tokens, upstream, row_factor, column_factor):
@@ -36,10 +40,7 @@
         "brcd,bscd->crs", upstream_cols, mixed_cols, preferred_element_type=jnp.float32
     )
     sum_row = jnp.einsum("brid,brjd->rij", back_rows, tokens, preferred_element_type=jnp.float32)
-    flat = jnp.concatenate([sum_row.reshape(-1), sum_column.reshape(-1)])
-    total = reduce_docs(flat, n)
-    split = sum_row.size
-    return (total[:split].reshape(sum_row.shape), total[split:].reshape(sum_column.shape))
+    return reduce_docs(sum_row, sum_column, n)
 
 
 def solution(mesh):

time: 151 us -> 144 us (0.954)
  other arithmetic: 7.15 us -> 1.14 us
    broadcast_in_dim x1 -> x0, other arithmetic: 3 us -> none  [reduce_docs(): spread = jnp.broadcast_to(mine[None], (n, mine.shape[0]))]
    all_to_all x1 -> x0, other arithmetic: 2.36 us -> none  [reduce_docs(): return lax.all_to_all(spread, 'dp', 0, 0, tiled=True).reshape(-1)]
    unnamed x12 -> x11, local copies, waits for them, and re-layouts: 4 us -> 3.81 us
where the time goes in v2:
time: 144 us
  blocking collectives  94.1 us (65%)
  waiting for transfers between devices  21.8 us (15%)
  starting transfers between devices  14.4 us (10%)
  local copies, waits for them, and re-layouts  10.2 us (7%)
  matrix products  1.55 us (1%)
    all_to_all x1, blocking collectives, shards(): lax.all_to_all(jnp.stack([send_m, send_b], 1), 'seq', 0, 0, tiled=True)  44.8 us
    all_to_all x1, blocking collectives, reduce_docs(): lax.all_to_all(flat, 'dp', 0, 0, tiled=True).sum(0).astype(jnp.bfloat16)  32.8 us
    all_to_all x1, waiting for transfers between devices, shards(): lax.all_to_all(upstream, 'seq', split_axis=2, concat_axis=1, tiled=True)  21.8 us
    all_to_all x1, blocking collectives, reduce_docs(): total = lax.all_to_all(spread, 'dp', 0, 0, tiled=True)  16.5 us
    all_to_all x1, starting transfers between devices, shards(): lax.all_to_all(upstream, 'seq', split_axis=2, concat_axis=1, tiled=True)  14.4 us
    unnamed x11, local copies, waits for them, and re-layouts  3.81 us
  transfers between devices with their start and end apart: 1, of which 1 were waited for; matrix products, arithmetic and copies ran while one was open for 1% of the time, Pallas kernels for 0%

profile of v2, /device:TPU:8, one launch (start us, length us, event | category | flops | bytes accessed | tf_op | source)
XLA Modules:
  0.0 143.8 jit_solution(17914479077159127677)
XLA Ops:
  0.6 0.0 copy-start
  0.6 0.0 copy-start.3
  0.7 2.9 %copy.16 = bf16[1,2,256,768]{3,1,0,2:T(2,128)(2,1)} copy(bf16[1,2,256,768]{3,2,1,0:T(8,128)(2,1)} %param.5) | data formatting | bytes 1572864 | tf_op args[1]
  3.6 14.4 %all-to-all-start = ((bf16[1,2,256,768]{3,1,0,2:T(2,128)(2,1)}), bf16[1,2,256,768]{3,1,0,2:T(2,128)(2,1)S(1)}, u32[]{:S(2)}, u32[]{:S(2)}) async-start(bf16[1,2,256,768]{3,1,0,2:T(2,128)(2,1)} %copy.16), calls=%async_computation | async-start | bytes 1572864 | tf_op jit(solution)/shard_map/all_to_all | solution.py:29
  17.9 0.0 copy-done
  18.0 0.0 copy-done.3
  18.0 0.4 fusion.1
  18.3 0.2 reshape_squeeze.4
  18.5 1.2 copy.31
  19.7 21.8 %all-to-all-done = bf16[1,2,256,768]{3,1,0,2:T(2,128)(2,1)S(1)} async-done(((bf16[1,2,256,768]{3,1,0,2:T(2,128)(2,1)}), bf16[1,2,256,768]{3,1,0,2:T(2,128)(2,1)S(1)}, u32[]{:S(2)}, u32[]{:S(2)}) %all-to-all-start) | async-done | bytes 786464 | tf_op jit(solution)/shard_map/all_to_all | solution.py:29
  41.5 0.0 copy-start.4
  41.5 0.5 copy.30
  42.0 0.3 reshape.43
  42.3 0.1 copy-done.4
  42.4 0.0 copy-start.1
  42.4 0.4 fusion
  42.8 0.6 copy.24
  43.4 0.1 copy-done.1
  43.5 1.0 pad_maximum_fusion
  44.5 44.8 %all_to_all.30 = bf16[64,2,2,4,768]{4,3,2,1,0:T(4,128)(2,1)S(1)} all-to-all(bf16[64,2,2,4,768]{4,3,2,1,0:T(4,128)(2,1)S(1)} %pad_maximum_fusion), channel_id=1, replica_groups=mesh['dp'=8,'seq'=64] {'seq'}, dimensions={0} | all-to-all | bytes 3145728 | tf_op jit(solution)/shard_map/all_to_all | solution.py:36
  89.3 1.4 slice_bitcast_fusion
  90.8 0.3 copy.20
  91.1 0.2 reshape.44
  91.2 0.0 copy-start.2
  91.3 0.4 fusion.3
  91.7 0.7 copy-done.2
  92.4 0.4 convolution_bitcast_fusion
  92.7 0.1 copy.22
  92.9 0.1 reshape.47
  93.0 0.1 pad_maximum_fusion.1
  93.1 32.8 %all_to_all.31 = f32[8,96,256]{2,1,0:T(8,128)S(1)} all-to-all(f32[8,96,256]{2,1,0:T(8,128)S(1)} %pad_maximum_fusion.1), channel_id=1, replica_groups=mesh['dp'=8,'seq'=64] {'dp'}, dimensions={0} | all-to-all | bytes 1572864 | tf_op jit(solution)/shard_map/all_to_all | solution.py:17
  125.8 0.1 reduce_sum.9
  125.9 16.5 %all_to_all.32 = bf16[8,96,256]{2,1,0:T(8,128)(2,1)S(1)} all-to-all(bf16[8,96,256]{2,1,0:T(8,128)(2,1)S(1)} %broadcast_in_dim.2), channel_id=1, replica_groups=mesh['dp'=8,'seq'=64] {'dp'}, dimensions={0} | all-to-all | bytes 786432 | tf_op jit(solution)/shard_map/all_to_all | solution.py:19
  142.4 0.7 reshape.49
  143.1 0.7 slice.18
  (2 shorter events, 0.0 us)
Async XLA Ops:
  0.6 17.3 %copy-start = (bf16[1,2,256,768]{3,2,1,0:T(8,128)(2,1)S(1)}, bf16[1,2,256,768]{3,2,1,0:T(8,128)(2,1)}, u32[]{:S(2)}) copy-start(bf16[1,2,256,768]{3,2,1,0:T(8,128)(2,1)} %param.4) | copy-start | bytes 2359300
  0.6 17.3 %copy-start.3 = (bf16[2,256,256]{2,1,0:T(8,128)(2,1)S(1)}, bf16[2,256,256]{2,1,0:T(8,128)(2,1)}, u32[]{:S(2)}) copy-start(bf16[2,256,256]{2,1,0:T(8,128)(2,1)} %param.6) | copy-start | bytes 786436
  3.6 37.9 %all-to-all-start = ((bf16[1,2,256,768]{3,1,0,2:T(2,128)(2,1)}), bf16[1,2,256,768]{3,1,0,2:T(2,128)(2,1)S(1)}, u32[]{:S(2)}, u32[]{:S(2)}) async-start(bf16[1,2,256,768]{3,1,0,2:T(2,128)(2,1)} %copy.16), calls=%async_computation | async-start | bytes 1572864 | tf_op jit(solution)/shard_map/all_to_all | solution.py:29
  41.5 0.9 copy-start.4
  42.4 1.1 copy-start.1
  91.2 1.1 copy-start.2

commit v3 on v1

v3 whole, which is shorter than its diff:
```python
import jax
import jax.numpy as jnp
from jax import lax
from jax.sharding import PartitionSpec as P

STAGES = (4, 2, 1)


def apply_rows(row_factor, tokens):
    return jnp.einsum(
        "rij,brjd->brid", row_factor, tokens, preferred_element_type=jnp.float32
    ).astype(jnp.bfloat16)


def halve_docs(part, n):
    q = lax.axis_index("dp")
    for bit in STAGES:
        half = part.shape[0] // 2
        mine = (q // bit) % 2
        keep = lax.dynamic_slice_in_dim(part, mine * half, half)
        give = lax.dynamic_slice_in_dim(part, (1 - mine) * half, half)
        part = keep + lax.ppermute(give, "dp", [(p, p ^ bit) for p in range(n)])
    return part


def shards(tokens, upstream, row_factor, column_factor):
    n = lax.psum(1, "dp")
    k = lax.psum(1, "seq")
    _, rows, cols, d = tokens.shape
    ncol = cols // k
    mixed = apply_rows(row_factor, tokens)
    send_u = upstream[0].reshape(rows, k, ncol, d).transpose(1, 0, 2, 3)
    send_m = mixed[0].reshape(rows, k, ncol, d).transpose(1, 0, 2, 3)
    got = lax.all_to_all(jnp.stack([send_u, send_m], 1), "seq", 0, 0, tiled=True)
    upstream_cols = got[:, 0].reshape(k * rows, ncol, d)
    mixed_cols = got[:, 1].reshape(k * rows, ncol, d)
    back_cols = jnp.einsum(
        "crs,rcd->scd", column_factor, upstream_cols, preferred_element_type=jnp.float32
    ).astype(jnp.bfloat16)
    back = lax.all_to_all(back_cols.reshape(k, rows, ncol, d), "seq", 0, 0, tiled=True)
    sum_column = jnp.einsum(
        "rcd,scd->crs", upstream_cols, mixed_cols, preferred_element_type=jnp.float32
    )
    width = cols
    col_part = halve_docs(sum_column.reshape(n, -1, width), n)
    col_part = col_part.astype(jnp.bfloat16).astype(jnp.float32)
    back_rows = back.transpose(1, 0, 2, 3).reshape(rows, cols, d)
    sum_row = jnp.einsum("rid,rjd->rij", back_rows, tokens[0], preferred_element_type=jnp.float32)
    row_parts = sum_row.reshape(n, -1, width)
    spread_col = jnp.broadcast_to(col_part, (n,) + col_part.shape[1:])
    got = lax.all_to_all(jnp.concatenate([row_parts, spread_col], 1), "dp", 0, 0, tiled=True)
    split = row_parts.shape[1]
    grad_column = got[:, split:].astype(jnp.bfloat16).reshape(sum_column.shape)
    row_mine = got[:, :split].sum(0).astype(jnp.bfloat16)
    total = lax.all_to_all(jnp.broadcast_to(row_mine[None], (n,) + row_mine.shape), "dp", 0, 0, tiled=True)
    return total.reshape(sum_row.shape), grad_column


def solution(mesh):
    placed = (
        P("dp", "seq", None, None),
        P("dp", "seq", None, None),
        P("seq", None, None),
        P("seq", None, None),
    )
    return jax.shard_map(
        shards,
        mesh=mesh,
        in_specs=placed,
        out_specs=(P("seq", None, None), P("seq", None, None)),
        check_vma=False,
    )
```

time: 151 us -> 144 us (0.954)
  blocking collectives: 94 us -> 84.1 us
  starting transfers between devices: 14.4 us -> 23.1 us
  other arithmetic: 7.15 us -> 2.36 us
  local copies, waits for them, and re-layouts: 10.6 us -> 8.82 us
    ppermute x0 -> x3, starting transfers between devices: none -> 13.4 us  [halve_docs(): part = keep + lax.ppermute(give, 'dp', [(p, p ^ bit) for p in range(n)])]
    all_to_all x1 -> x2, waiting for transfers between devices: 21.8 us -> 10.4 us  [the longest x1 10.4 us: shards(): lax.all_to_all(jnp.broadcast_to(row_mine[None], (n,) + row_mine.shape), '...]
    ppermute x0 -> x3, waiting for transfers between devices: none -> 11.3 us  [halve_docs(): part = keep + lax.ppermute(give, 'dp', [(p, p ^ bit) for p in range(n)])]
    all_to_all x3 -> x2, blocking collectives: 94 us -> 84.1 us  [the longest x1 53.7 us: shards(): lax.all_to_all(jnp.stack([send_u, send_m], 1), 'seq', 0, 0, tiled=True)]
    all_to_all x1 -> x2, starting transfers between devices: 14.4 us -> 9.77 us  [the longest x1 6.36 us: shards(): lax.all_to_all(back_cols.reshape(k, rows, ncol, d), 'seq', 0, 0, tiled=True)]
    broadcast_in_dim x1, other arithmetic: 3 us -> 0.01 us  [shards(): spread_col = jnp.broadcast_to(col_part, (n,) + col_part.shape[1:])]
    reshape x0 -> x4, local copies, waits for them, and re-layouts: none -> 2.53 us  [the longest x2 1.75 us: shards(): back_cols.reshape(k, rows, ncol, d)]
    all_to_all x1 -> x0, other arithmetic: 2.36 us -> none  [reduce_docs(): return lax.all_to_all(spread, 'dp', 0, 0, tiled=True).reshape(-1)]
  transfers between devices with their start and end apart: 1 -> 5, of which waited for: 1 -> 4; matrix products, arithmetic and copies ran while one was open for 1% -> 1% of each run, Pallas kernels for 0% -> 0%
where the time goes in v3:
time: 144 us
  blocking collectives  84.1 us (58%)
  starting transfers between devices  23.1 us (16%)
  waiting for transfers between devices  21.7 us (15%)
  local copies, waits for them, and re-layouts  8.82 us (6%)
  matrix products  2.51 us (2%)
  other arithmetic  2.36 us (2%)
    all_to_all x1, blocking collectives, shards(): lax.all_to_all(jnp.stack([send_u, send_m], 1), 'seq', 0, 0, tiled=True)  53.7 us
    all_to_all x1, blocking collectives, shards(): lax.all_to_all(jnp.concatenate([row_parts, spread_col], 1), 'dp', 0, 0, t...  30.4 us
    ppermute x3, starting transfers between devices, halve_docs(): part = keep + lax.ppermute(give, 'dp', [(p, p ^ bit) for p in range(n)])  13.4 us
    ppermute x3, waiting for transfers between devices, halve_docs(): part = keep + lax.ppermute(give, 'dp', [(p, p ^ bit) for p in range(n)])  11.3 us
    all_to_all x1, waiting for transfers between devices, shards(): lax.all_to_all(jnp.broadcast_to(row_mine[None], (n,) + row_mine.shape), '...  10.4 us
    all_to_all x1, starting transfers between devices, shards(): lax.all_to_all(back_cols.reshape(k, rows, ncol, d), 'seq', 0, 0, tiled=True)  6.36 us
    all_to_all x1, starting transfers between devices, shards(): lax.all_to_all(jnp.broadcast_to(row_mine[None], (n,) + row_mine.shape), '...  3.41 us
  transfers between devices with their start and end apart: 5, of which 4 were waited for; matrix products, arithmetic and copies ran while one was open for 1% of the time, Pallas kernels for 0%

profile of v3, /device:TPU:8, one launch (start us, length us, event | category | flops | bytes accessed | tf_op | source)
XLA Modules:
  0.0 143.7 jit_solution(8481758213631985548)
XLA Ops:
  0.6 0.0 copy-start
  0.6 0.0 copy-start.1
  0.7 1.1 copy-done
  1.8 1.3 fusion.1
  3.1 0.8 copy.25
  3.9 0.0 copy-done.1
  3.9 0.8 copy.16
  4.7 2.2 %pad_maximum_fusion = bf16[64,2,2,4,768]{4,2,3,0,1:T(2,128)(2,1)S(1)} fusion(bf16[64,1,2,4,768]{4,2,3,0,1:T(2,128)(2,1)S(1)} %bitcast.37, bf16[64,1,2,4,768]{4,2,3,0,1:T(2,128)(2,1)S(1)} %bitcast.38), kind=kLoop, calls=%fused_computation | loop fusion | flops 786432 | bytes 3145728 | tf_op jit(solution)/shard_map/stack | solution.py:34
  7.0 0.6 copy.18
  7.6 53.7 %all_to_all.20 = bf16[64,2,2,4,768]{4,3,2,1,0:T(4,128)(2,1)S(1)} all-to-all(bf16[64,2,2,4,768]{4,3,2,1,0:T(4,128)(2,1)S(1)} %copy.18), channel_id=1, replica_groups=mesh['dp'=8,'seq'=64] {'seq'}, dimensions={0} | all-to-all | bytes 3145728 | tf_op jit(solution)/shard_map/all_to_all | solution.py:34
  61.3 0.0 copy-start.3
  61.3 1.4 fusion.12
  62.7 0.0 copy-done.3
  62.8 0.4 fusion
  63.2 0.3 reshape.31
  63.5 0.0 copy-start.2
  63.5 1.5 %copy.21 = bf16[64,2,4,768]{3,1,2,0:T(2,128)(2,1)} copy(bf16[64,2,4,768]{3,1,0,2:T(2,128)(2,1)S(1)} %reshape.31) | data formatting | bytes 1572864 | tf_op jit(solution)/shard_map/reshape | solution.py:40
  64.9 6.4 %all-to-all-start.1 = ((bf16[64,2,4,768]{3,1,2,0:T(2,128)(2,1)}), bf16[64,2,4,768]{3,1,2,0:T(2,128)(2,1)S(1)}, u32[]{:S(2)}, u32[]{:S(2)}) async-start(bf16[64,2,4,768]{3,1,2,0:T(2,128)(2,1)} %copy.21), calls=%async_computation.1 | async-start | bytes 1572864 | tf_op jit(solution)/shard_map/all_to_all | solution.py:40
  71.3 0.0 copy-done.2
  71.3 0.4 fusion.2
  71.7 0.1 reshape.34
  71.8 4.9 %collective-permute-start = (f32[4,32,256]{2,1,0:T(8,128)S(1)}, f32[4,32,256]{2,1,0:T(8,128)S(1)}, u32[]{:S(2)}, u32[]{:S(2)}) collective-permute-start(f32[4,32,256]{2,1,0:T(8,128)S(1)} %constant_dynamic-slice_fusion.2), channel_id=1, source_target_pairs={{0,256},{64,320},{128,384},{192,448},{256,0},{320,64},{384,128},{4... | collective-permute-start | bytes 393224 | tf_op jit(solution)/shard_map/ppermute | solution.py:22
  76.8 3.9 %collective-permute-done = f32[4,32,256]{2,1,0:T(8,128)S(1)} collective-permute-done((f32[4,32,256]{2,1,0:T(8,128)S(1)}, f32[4,32,256]{2,1,0:T(8,128)S(1)}, u32[]{:S(2)}, u32[]{:S(2)}) %collective-permute-start) | collective-permute-done | bytes 131104 | tf_op jit(solution)/shard_map/ppermute | solution.py:22
  80.8 3.4 %collective-permute-start.1 = (f32[2,32,256]{2,1,0:T(8,128)S(1)}, f32[2,32,256]{2,1,0:T(8,128)S(1)}, u32[]{:S(2)}, u32[]{:S(2)}) collective-permute-start(f32[2,32,256]{2,1,0:T(8,128)S(1)} %constant_dynamic-slice_fusion.1), channel_id=1, source_target_pairs={{0,128},{64,192},{128,0},{192,64},{256,384},{320,448},{384,256},{4... | collective-permute-start | bytes 196616 | tf_op jit(solution)/shard_map/ppermute | solution.py:22
  84.2 2.7 %collective-permute-done.1 = f32[2,32,256]{2,1,0:T(8,128)S(1)} collective-permute-done((f32[2,32,256]{2,1,0:T(8,128)S(1)}, f32[2,32,256]{2,1,0:T(8,128)S(1)}, u32[]{:S(2)}, u32[]{:S(2)}) %collective-permute-start.1) | collective-permute-done | bytes 65568 | tf_op jit(solution)/shard_map/ppermute | solution.py:22
  87.0 5.0 %collective-permute-start.2 = (f32[1,32,256]{2,1,0:T(8,128)S(1)}, f32[1,32,256]{2,1,0:T(8,128)S(1)}, u32[]{:S(2)}, u32[]{:S(2)}) collective-permute-start(f32[1,32,256]{2,1,0:T(8,128)S(1)} %constant_dynamic-slice_fusion), channel_id=1, source_target_pairs={{0,64},{64,0},{128,192},{192,128},{256,320},{320,256},{384,448},{4... | collective-permute-start | bytes 98312 | tf_op jit(solution)/shard_map/ppermute | solution.py:22
  92.0 4.7 %collective-permute-done.2 = f32[1,32,256]{2,1,0:T(8,128)S(1)} collective-permute-done((f32[1,32,256]{2,1,0:T(8,128)S(1)}, f32[1,32,256]{2,1,0:T(8,128)S(1)}, u32[]{:S(2)}, u32[]{:S(2)}) %collective-permute-start.2) | collective-permute-done | bytes 32800 | tf_op jit(solution)/shard_map/ppermute | solution.py:22
  96.7 0.0 all-to-all-done.1
  96.7 0.4 fusion.4
  97.2 0.1 pad_maximum_fusion.1
  97.2 30.4 %all_to_all.21 = f32[8,96,256]{2,1,0:T(8,128)S(1)} all-to-all(f32[8,96,256]{2,1,0:T(8,128)S(1)} %pad_maximum_fusion.1), channel_id=1, replica_groups=mesh['dp'=8,'seq'=64] {'dp'}, dimensions={0} | all-to-all | bytes 1572864 | tf_op jit(solution)/shard_map/all_to_all | solution.py:51
  127.7 0.7 broadcast_in_dim.19
  128.4 3.4 %all-to-all-start.3 = ((bf16[8,64,256]{2,1,0:T(8,128)(2,1)}), bf16[8,64,256]{2,1,0:T(8,128)(2,1)S(1)}, u32[]{:S(2)}, u32[]{:S(2)}) async-start(bf16[8,64,256]{2,1,0:T(8,128)(2,1)} %broadcast_in_dim.19), calls=%async_computation.3 | async-start | bytes 524288 | tf_op jit(solution)/shard_map/all_to_all | solution.py:55
  131.9 0.7 reshape.36
  132.6 10.4 %all-to-all-done.3 = bf16[8,64,256]{2,1,0:T(8,128)(2,1)S(1)} async-done(((bf16[8,64,256]{2,1,0:T(8,128)(2,1)}), bf16[8,64,256]{2,1,0:T(8,128)(2,1)S(1)}, u32[]{:S(2)}, u32[]{:S(2)}) %all-to-all-start.3) | async-done | bytes 262176 | tf_op jit(solution)/shard_map/all_to_all | solution.py:55
  143.0 0.7 copy.38
  (9 shorter events, 0.1 us)
Async XLA Ops:
  0.6 1.1 copy-start
  0.6 3.3 %copy-start.1 = (bf16[1,2,256,768]{3,2,1,0:T(8,128)(2,1)S(1)}, bf16[1,2,256,768]{3,2,1,0:T(8,128)(2,1)}, u32[]{:S(2)}) copy-start(bf16[1,2,256,768]{3,2,1,0:T(8,128)(2,1)} %param.5) | copy-start | bytes 2359300
  61.3 1.4 copy-start.3
  63.5 7.9 %copy-start.2 = (bf16[64,1,2,4,768]{4,3,2,1,0:T(4,128)(2,1)S(1)}, bf16[64,1,2,4,768]{4,3,2,1,0:T(4,128)(2,1)}, u32[]{:S(2)}) copy-start(bf16[64,1,2,4,768]{4,3,2,1,0:T(4,128)(2,1)} %get-tuple-element.3) | copy-start | bytes 2359300
  64.9 31.8 %all-to-all-start.1 = ((bf16[64,2,4,768]{3,1,2,0:T(2,128)(2,1)}), bf16[64,2,4,768]{3,1,2,0:T(2,128)(2,1)S(1)}, u32[]{:S(2)}, u32[]{:S(2)}) async-start(bf16[64,2,4,768]{3,1,2,0:T(2,128)(2,1)} %copy.21), calls=%async_computation.1 | async-start | bytes 1572864 | tf_op jit(solution)/shard_map/all_to_all | solution.py:40
  71.8 8.9 %collective-permute-start = (f32[4,32,256]{2,1,0:T(8,128)S(1)}, f32[4,32,256]{2,1,0:T(8,128)S(1)}, u32[]{:S(2)}, u32[]{:S(2)}) collective-permute-start(f32[4,32,256]{2,1,0:T(8,128)S(1)} %constant_dynamic-slice_fusion.2), channel_id=1, source_target_pairs={{0,256},{64,320},{128,384},{192,448},{256,0},{320,64},{384,128},{4... | collective-permute-start | bytes 393224 | tf_op jit(solution)/shard_map/ppermute | solution.py:22
  80.8 6.2 %collective-permute-start.1 = (f32[2,32,256]{2,1,0:T(8,128)S(1)}, f32[2,32,256]{2,1,0:T(8,128)S(1)}, u32[]{:S(2)}, u32[]{:S(2)}) collective-permute-start(f32[2,32,256]{2,1,0:T(8,128)S(1)} %constant_dynamic-slice_fusion.1), channel_id=1, source_target_pairs={{0,128},{64,192},{128,0},{192,64},{256,384},{320,448},{384,256},{4... | collective-permute-start | bytes 196616 | tf_op jit(solution)/shard_map/ppermute | solution.py:22
  87.0 9.7 %collective-permute-start.2 = (f32[1,32,256]{2,1,0:T(8,128)S(1)}, f32[1,32,256]{2,1,0:T(8,128)S(1)}, u32[]{:S(2)}, u32[]{:S(2)}) collective-permute-start(f32[1,32,256]{2,1,0:T(8,128)S(1)} %constant_dynamic-slice_fusion), channel_id=1, source_target_pairs={{0,64},{64,0},{128,192},{192,128},{256,320},{320,256},{384,448},{4... | collective-permute-start | bytes 98312 | tf_op jit(solution)/shard_map/ppermute | solution.py:22
  128.4 14.5 %all-to-all-start.3 = ((bf16[8,64,256]{2,1,0:T(8,128)(2,1)}), bf16[8,64,256]{2,1,0:T(8,128)(2,1)S(1)}, u32[]{:S(2)}, u32[]{:S(2)}) async-start(bf16[8,64,256]{2,1,0:T(8,128)(2,1)} %broadcast_in_dim.19), calls=%async_computation.3 | async-start | bytes 524288 | tf_op jit(solution)/shard_map/all_to_all | solution.py:55
